TPU v7x, 512 devices: a whole 4x4x16 slice. The times are simulated.
512 devices in a mesh: patch: 16 (over y, x_hi, core), map: 32 (over x_lo, z).
Axes of the slice: x: 4 (x_hi: 2, x_lo: 2; x = x_hi * 2 + x_lo), y: 4, z: 16, core: 2. Of those that a mesh axis runs over, the one named last changes fastest.
Arguments:
- maps: bfloat16 [64, 32, 24576], P('map', None, 'patch'), may hold values from -6 to 6
- cotangent: bfloat16 [64, 32, 24576], P('map', None, 'patch'), may hold values from -6 to 6
- tiles: bfloat16 [96, 3, 256, 256], P('patch'), may hold values from -0.21875 to 0.21875
- columns: int32 [96, 3], P('patch'), may hold values from 0 to 95, as said below
- filters: bfloat16 [3, 32, 32], replicated, may hold values from -0.625 to 0.625
Outputs:
- output: bfloat16 [64, 32, 24576], P('map', None, 'patch')
- input_grad: bfloat16 [64, 32, 24576], P('map', None, 'patch')
- filter_grad: float32 [3, 32, 32], replicated
Inputs may be any that keep to these rules, and one draw needn't show every extreme that they name: `columns`: slot 0 of block row b names block b itself, slot 1 a block 1 to 2 before it and slot 2 a block 1 to 2 after it, counted cyclically over the 96 blocks; block row 0 reads exactly 2 blocks away on both sides.
All inputs are finite; a program needn't handle non-finite values.
Results may differ from a plain program's by a relative error of at most 0.0054.
Values may be sent and summed in bfloat16 or wider, within the bound.
No kernel may reach another device: no remote copies, remote signals or barrier semaphores. Data moves between devices by JAX's collectives and lax.ppermute only.
A program may use at most 64 MiB of HBM per device.

v0:
```python
import math
import jax
import jax.numpy as jnp
from jax import lax
from jax.sharding import PartitionSpec as P

REACH = 2


def extended_2(cells, sides, width):
    for axis, dim in sides:
        count = lax.axis_size(axis)
        head = lax.slice_in_dim(cells, 0, width, axis=dim)
        tail = lax.slice_in_dim(cells, cells.shape[dim] - width, cells.shape[dim], axis=dim)
        cells = jnp.concatenate(
            [
                lax.ppermute(tail, axis, [(i, (i + 1) % count) for i in range(count)]),
                cells,
                lax.ppermute(head, axis, [((i + 1) % count, i) for i in range(count)]),
            ],
            axis=dim,
        )
    return cells


def offset_sums(grad_blocks, tile_set, offset_mask):
    contrib = jnp.einsum(
        "nui,ujiq->nujq", grad_blocks, tile_set, preferred_element_type=jnp.float32
    )
    return jnp.einsum(
        "uje,nujq->nueq", offset_mask.astype(jnp.float32), contrib, precision=lax.Precision.HIGHEST
    )


def per_device(maps, cotangent, tiles, columns, filters):
    map_count = maps.shape[0]
    chan_count = maps.shape[1]
    pix_count = maps.shape[2]
    block_count = tiles.shape[0]
    block_size = tiles.shape[2]
    reach_blocks = REACH
    spread = 2 * reach_blocks + 1
    row_count = map_count * chan_count
    rim_cells = reach_blocks * block_size
    patch_count = lax.axis_size("patch")
    total_blocks = block_count * patch_count
    first_block = lax.axis_index("patch") * block_count
    row_ids = first_block + jnp.arange(block_count, dtype=jnp.int32)
    offset_ids = jnp.arange(spread, dtype=jnp.int32)
    own_offset = (columns - row_ids[:, None] + reach_blocks) % total_blocks
    own_mask = own_offset[:, :, None] == offset_ids[None, None, :]

    def forward_apply(field):
        extended = extended_2(field, (("patch", 2),), rim_cells)
        ext_blocks = extended.reshape(row_count, block_count + 2 * reach_blocks, block_size)
        shifted = jnp.stack(
            [ext_blocks[:, offset : offset + block_count] for offset in range(spread)], axis=2
        )
        picked = jnp.einsum(
            "rje,nreq->nrjq",
            own_mask.astype(jnp.bfloat16),
            shifted,
            preferred_element_type=jnp.bfloat16,
        )
        result = jnp.einsum("nrjq,rjiq->nri", picked, tiles, preferred_element_type=jnp.float32)
        return result.reshape(map_count, chan_count, pix_count)

    def adjoint_apply(grads):
        by_offset = offset_sums(grads.reshape(row_count, block_count, block_size), tiles, own_mask)
        window = jnp.pad(by_offset[:, :, 0], ((0, 0), (0, spread - 1), (0, 0)))
        for offset in range(1, spread):
            window = window + jnp.pad(
                by_offset[:, :, offset], ((0, 0), (offset, spread - 1 - offset), (0, 0))
            )
        own_part = window[:, reach_blocks : reach_blocks + block_count]
        outgoing = jnp.concatenate(
            [window[:, :reach_blocks], window[:, reach_blocks + block_count :]], axis=1
        )
        outgoing = outgoing.reshape(map_count, chan_count, 2 * rim_cells)
        incoming = extended_2(outgoing, (("patch", 2),), rim_cells)
        from_left = incoming[:, :, :rim_cells].reshape(row_count, reach_blocks, block_size)
        from_right = incoming[:, :, incoming.shape[2] - rim_cells :].reshape(
            row_count, reach_blocks, block_size
        )
        own_part = own_part.at[:, :reach_blocks].add(from_left)
        own_part = own_part.at[:, block_count - reach_blocks :].add(from_right)
        return own_part.reshape(map_count, chan_count, pix_count)

    x_one = forward_apply(maps).astype(jnp.bfloat16)
    x_two = (2.0 * forward_apply(x_one) - maps.astype(jnp.float32)).astype(jnp.bfloat16)
    terms = jnp.stack([maps, x_one, x_two])
    output = jnp.einsum("kco,kmcp->mop", filters, terms, preferred_element_type=jnp.float32).astype(
        jnp.bfloat16
    )
    grads = jnp.einsum("kco,mop->kmcp", filters, cotangent, preferred_element_type=jnp.float32)
    grad_two = grads[2].astype(jnp.bfloat16)
    update = (grads[1] + 2.0 * adjoint_apply(grad_two)).astype(jnp.bfloat16)
    input_grad = (grads[0] - grad_two.astype(jnp.float32) + adjoint_apply(update)).astype(
        jnp.bfloat16
    )
    scale = 1.0 / math.sqrt(map_count * lax.axis_size("map") * pix_count * patch_count)
    local_grad = jnp.einsum("kmcp,mop->kco", terms, cotangent, preferred_element_type=jnp.float32)
    filter_grad = lax.psum(local_grad, ("patch", "map")) * scale
    return (output, input_grad, filter_grad)


def solution(mesh):
    placed = (
        P("map", None, "patch"),
        P("map", None, "patch"),
        P("patch", None, None, None),
        P("patch", None),
        P(),
    )
    return jax.shard_map(
        per_device,
        mesh=mesh,
        in_specs=placed,
        out_specs=(P("map", None, "patch"), P("map", None, "patch"), P()),
        check_vma=False,
    )
```

profile of v0, /device:TPU:1, one launch (start us, length us, event | category | flops | bytes accessed | tf_op | source)
XLA Modules:
  0.0 221.6 jit_solution(9846326644404595408)
XLA Ops:
  4.6 2.3 %convolution_bitcast_fusion.3 = f32[64,6,5,256]{3,2,0,1:T(8,128)S(1)} fusion(f32[6,64,3,256]{3,1,2,0:T(8,128)S(1)} %fusion.38, s32[6,3]{1,0:T(8,128)S(1)} %copy.21), kind=kOutput, calls=%fused_computation.5 | convolution fusion | flops 17694810 | bytes 3145800 | tf_op jit(solution)/shard_map/uje,nujq->nueq/dot_general | solution.py:30
  6.9 1.8 fusion.56
  10.8 1.8 reshape.181
  12.6 1.8 fusion.58
  14.4 6.0 %collective-permute-start.4 = (f32[2,32,512]{2,1,0:T(8,128)}, f32[2,32,512]{2,1,0:T(8,128)}, u32[]{:S(2)}, u32[]{:S(2)}) collective-permute-start(f32[2,32,512]{2,1,0:T(8,128)} %get-tuple-element.68), channel_id=1, source_target_pairs={{0,32},{32,64},{64,96},{96,128},{128,160},{160,192},{192,224},{224... | collective-permute-start | bytes 393224 | tf_op jit(solution)/shard_map/ppermute | solution.py:17
  20.4 4.7 %collective-permute-start.5 = (f32[2,32,512]{2,1,0:T(8,128)}, f32[2,32,512]{2,1,0:T(8,128)}, u32[]{:S(2)}, u32[]{:S(2)}) collective-permute-start(f32[2,32,512]{2,1,0:T(8,128)} %get-tuple-element.67), channel_id=1, source_target_pairs={{32,0},{64,32},{96,64},{128,96},{160,128},{192,160},{224,192},{256... | collective-permute-start | bytes 393224 | tf_op jit(solution)/shard_map/ppermute | solution.py:19
  26.6 2.4 %collective-permute-start = (bf16[2,32,512]{2,1,0:T(8,128)(2,1)}, bf16[2,32,512]{2,1,0:T(8,128)(2,1)}, u32[]{:S(2)}, u32[]{:S(2)}) collective-permute-start(bf16[2,32,512]{2,1,0:T(8,128)(2,1)} %get-tuple-element.71), channel_id=1, source_target_pairs={{0,32},{32,64},{64,96},{96,128},{128,160},{160,192},{192,224},{224... | collective-permute-start | bytes 196616 | tf_op jit(solution)/shard_map/ppermute | solution.py:17
  29.0 6.8 %collective-permute-start.1 = (bf16[2,32,512]{2,1,0:T(8,128)(2,1)}, bf16[2,32,512]{2,1,0:T(8,128)(2,1)}, u32[]{:S(2)}, u32[]{:S(2)}) collective-permute-start(bf16[2,32,512]{2,1,0:T(8,128)(2,1)} %get-tuple-element.72), channel_id=1, source_target_pairs={{32,0},{64,32},{96,64},{128,96},{160,128},{192,160},{224,192},{256... | collective-permute-start | bytes 196616 | tf_op jit(solution)/shard_map/ppermute | solution.py:19
  35.8 1.8 slice.264
  38.5 1.9 squeeze.35
  46.6 1.9 convert_element_type.73
  48.4 1.9 convert_element_type.72
  51.8 1.9 collective-permute-start.2
  53.7 7.4 %collective-permute-start.3 = (bf16[2,32,512]{2,1,0:T(8,128)(2,1)}, bf16[2,32,512]{2,1,0:T(8,128)(2,1)}, u32[]{:S(2)}, u32[]{:S(2)}) collective-permute-start(bf16[2,32,512]{2,1,0:T(8,128)(2,1)} %get-tuple-element.70), channel_id=1, source_target_pairs={{32,0},{64,32},{96,64},{128,96},{160,128},{192,160},{224,192},{256... | collective-permute-start | bytes 196616 | tf_op jit(solution)/shard_map/ppermute | solution.py:19
  61.2 1.6 reshape.182
  62.8 1.7 fusion.44
  67.1 1.6 fusion.34
  68.7 2.3 %convolution_bitcast_fusion.2 = f32[64,6,5,256]{3,2,0,1:T(8,128)S(1)} fusion(f32[6,64,3,256]{3,1,2,0:T(8,128)S(1)} %fusion.34, s32[6,3]{1,0:T(8,128)S(1)} %copy.21), kind=kOutput, calls=%fused_computation.4 | convolution fusion | flops 17694810 | bytes 3145800 | tf_op jit(solution)/shard_map/uje,nujq->nueq/dot_general | solution.py:30
  71.0 1.8 fusion.55
  82.8 2.0 convolution_bitcast_fusion.6
  86.7 1.8 reshape.184
  88.4 1.7 fusion.57
  90.1 1.9 collective-permute-start.6
  92.0 1.8 slice.279
  93.8 7.2 %collective-permute-start.7 = (f32[2,32,512]{2,1,0:T(8,128)}, f32[2,32,512]{2,1,0:T(8,128)}, u32[]{:S(2)}, u32[]{:S(2)}) collective-permute-start(f32[2,32,512]{2,1,0:T(8,128)} %get-tuple-element.65), channel_id=1, source_target_pairs={{32,0},{64,32},{96,64},{128,96},{160,128},{192,160},{224,192},{256... | collective-permute-start | bytes 393224 | tf_op jit(solution)/shard_map/ppermute | solution.py:19
  101.0 106.8 %psum.7 = f32[3,32,32]{2,1,0:T(8,128)} all-reduce(f32[3,32,32]{2,1,0:T(8,128)} %convolution_bitcast_fusion.6), channel_id=1, replica_groups=mesh['patch'=16,'map'=32] {'patch','map'}, use_global_device_ids=true, to_apply=%region_0.1 | all-reduce | flops 3072 | bytes 24576 | tf_op jit(solution)/shard_map/psum | solution.py:103
  209.2 1.6 reshape.185
  210.9 1.7 fusion.42
  212.5 1.7 reshape.186
  215.9 2.0 copy.42
  218.0 1.9 reshape.187
  219.9 1.7 fusion.20
  (109 shorter events, 33.2 us)
Async XLA Ops:
  0.6 3.5 %copy-start = (bf16[6,3,256,256]{3,2,1,0:T(8,128)(2,1)S(1)}, bf16[6,3,256,256]{3,2,1,0:T(8,128)(2,1)}, u32[]{:S(2)}) copy-start(bf16[6,3,256,256]{3,2,1,0:T(8,128)(2,1)} %param.15) | copy-start | bytes 7077892
  2.8 1.0 copy-start.15
  8.9 28.7 %copy-start.7 = (f32[64,6,256]{2,0,1:T(8,128)}, f32[64,6,256]{2,0,1:T(8,128)S(1)}, u32[]{:S(2)}) copy-start(f32[64,6,256]{2,0,1:T(8,128)S(1)} %get-tuple-element.73) | copy-start | bytes 1179652
  8.9 28.7 %copy-start.9 = (f32[64,6,256]{2,0,1:T(8,128)}, f32[64,6,256]{2,0,1:T(8,128)S(1)}, u32[]{:S(2)}) copy-start(f32[64,6,256]{2,0,1:T(8,128)S(1)} %get-tuple-element.74) | copy-start | bytes 1179652
  9.0 0.8 copy-start.11
  9.0 1.0 copy-start.13
  12.6 25.0 %copy-start.12 = (f32[64,6,256]{2,0,1:T(8,128)S(1)}, f32[64,6,256]{2,0,1:T(8,128)}, u32[]{:S(2)}) copy-start(f32[64,6,256]{2,0,1:T(8,128)} %copy-done.11) | copy-start | bytes 1179652
  12.6 25.0 %copy-start.14 = (f32[64,6,256]{2,0,1:T(8,128)S(1)}, f32[64,6,256]{2,0,1:T(8,128)}, u32[]{:S(2)}) copy-start(f32[64,6,256]{2,0,1:T(8,128)} %copy-done.13) | copy-start | bytes 1179652
  14.4 46.8 %collective-permute-start.4 = (f32[2,32,512]{2,1,0:T(8,128)}, f32[2,32,512]{2,1,0:T(8,128)}, u32[]{:S(2)}, u32[]{:S(2)}) collective-permute-start(f32[2,32,512]{2,1,0:T(8,128)} %get-tuple-element.68), channel_id=1, source_target_pairs={{0,32},{32,64},{64,96},{96,128},{128,160},{160,192},{192,224},{224... | collective-permute-start | bytes 393224 | tf_op jit(solution)/shard_map/ppermute | solution.py:17
  20.4 44.1 %collective-permute-start.5 = (f32[2,32,512]{2,1,0:T(8,128)}, f32[2,32,512]{2,1,0:T(8,128)}, u32[]{:S(2)}, u32[]{:S(2)}) collective-permute-start(f32[2,32,512]{2,1,0:T(8,128)} %get-tuple-element.67), channel_id=1, source_target_pairs={{32,0},{64,32},{96,64},{128,96},{160,128},{192,160},{224,192},{256... | collective-permute-start | bytes 393224 | tf_op jit(solution)/shard_map/ppermute | solution.py:19
  26.6 13.8 %collective-permute-start = (bf16[2,32,512]{2,1,0:T(8,128)(2,1)}, bf16[2,32,512]{2,1,0:T(8,128)(2,1)}, u32[]{:S(2)}, u32[]{:S(2)}) collective-permute-start(bf16[2,32,512]{2,1,0:T(8,128)(2,1)} %get-tuple-element.71), channel_id=1, source_target_pairs={{0,32},{32,64},{64,96},{96,128},{128,160},{160,192},{192,224},{224... | collective-permute-start | bytes 196616 | tf_op jit(solution)/shard_map/ppermute | solution.py:17
  29.0 11.4 %collective-permute-start.1 = (bf16[2,32,512]{2,1,0:T(8,128)(2,1)}, bf16[2,32,512]{2,1,0:T(8,128)(2,1)}, u32[]{:S(2)}, u32[]{:S(2)}) collective-permute-start(bf16[2,32,512]{2,1,0:T(8,128)(2,1)} %get-tuple-element.72), channel_id=1, source_target_pairs={{32,0},{64,32},{96,64},{128,96},{160,128},{192,160},{224,192},{256... | collective-permute-start | bytes 196616 | tf_op jit(solution)/shard_map/ppermute | solution.py:19
  37.7 2.7 %copy-start.18 = (bf16[2,32,1536]{2,1,0:T(8,128)(2,1)S(1)}, bf16[2,32,1536]{2,1,0:T(8,128)(2,1)}, u32[]{:S(2)}) copy-start(bf16[2,32,1536]{2,1,0:T(8,128)(2,1)} %param.13) | copy-start | bytes 589828
  45.7 17.1 %copy-start.8 = (f32[64,6,256]{2,0,1:T(8,128)S(1)}, f32[64,6,256]{2,0,1:T(8,128)}, u32[]{:S(2)}) copy-start(f32[64,6,256]{2,0,1:T(8,128)} %copy-done.7) | copy-start | bytes 1179652
  45.7 17.1 %copy-start.10 = (f32[64,6,256]{2,0,1:T(8,128)S(1)}, f32[64,6,256]{2,0,1:T(8,128)}, u32[]{:S(2)}) copy-start(f32[64,6,256]{2,0,1:T(8,128)} %copy-done.9) | copy-start | bytes 1179652
  51.8 23.2 %collective-permute-start.2 = (bf16[2,32,512]{2,1,0:T(8,128)(2,1)}, bf16[2,32,512]{2,1,0:T(8,128)(2,1)}, u32[]{:S(2)}, u32[]{:S(2)}) collective-permute-start(bf16[2,32,512]{2,1,0:T(8,128)(2,1)} %get-tuple-element.69), channel_id=1, source_target_pairs={{0,32},{32,64},{64,96},{96,128},{128,160},{160,192},{192,224},{224... | collective-permute-start | bytes 196616 | tf_op jit(solution)/shard_map/ppermute | solution.py:17
  53.7 21.3 %collective-permute-start.3 = (bf16[2,32,512]{2,1,0:T(8,128)(2,1)}, bf16[2,32,512]{2,1,0:T(8,128)(2,1)}, u32[]{:S(2)}, u32[]{:S(2)}) collective-permute-start(bf16[2,32,512]{2,1,0:T(8,128)(2,1)} %get-tuple-element.70), channel_id=1, source_target_pairs={{32,0},{64,32},{96,64},{128,96},{160,128},{192,160},{224,192},{256... | collective-permute-start | bytes 196616 | tf_op jit(solution)/shard_map/ppermute | solution.py:19
  72.9 1.3 copy-start.1
  73.0 1.3 copy-start.3
  73.0 1.3 copy-start.5
  73.0 1.2 copy-start.6
  74.3 1.0 copy-start.17
  80.6 1.1 copy-start.19
  81.7 3.1 %copy-start.22 = (bf16[1,2,32,1536]{3,2,1,0:T(8,128)(2,1)S(1)}, bf16[1,2,32,1536]{3,2,1,0:T(8,128)(2,1)}, u32[]{:S(2)}) copy-start(bf16[1,2,32,1536]{3,2,1,0:T(8,128)(2,1)} %convert_element_type.72) | copy-start | bytes 589828
  81.7 3.1 %copy-start.23 = (bf16[3,32,32]{2,1,0:T(8,128)(2,1)S(1)}, bf16[3,32,32]{2,1,0:T(8,128)(2,1)}, u32[]{:S(2)}) copy-start(bf16[3,32,32]{2,1,0:T(8,128)(2,1)} %param.17) | copy-start | bytes 18436
  82.8 3.0 %copy-start.20 = (f32[64,2,256]{2,0,1:T(8,128)S(1)}, f32[64,2,256]{2,0,1:T(8,128)}, u32[]{:S(2)}) copy-start(f32[64,2,256]{2,0,1:T(8,128)} %get-tuple-element.61) | copy-start | bytes 393220
  82.8 3.0 %copy-start.21 = (f32[64,2,256]{2,0,1:T(8,128)S(1)}, f32[64,2,256]{2,0,1:T(8,128)}, u32[]{:S(2)}) copy-start(f32[64,2,256]{2,0,1:T(8,128)} %get-tuple-element.62) | copy-start | bytes 393220
  85.8 125.1 %copy-start.2 = (f32[64,6,1,256]{3,0,1,2:T(8,128)S(1)}, f32[64,6,1,256]{3,0,1,2:T(8,128)}, u32[]{:S(2)}) copy-start(f32[64,6,1,256]{3,0,1,2:T(8,128)} %copy-done.1) | copy-start | bytes 1179652
  85.8 125.1 %copy-start.4 = (f32[64,6,1,256]{3,0,1,2:T(8,128)S(1)}, f32[64,6,1,256]{3,0,1,2:T(8,128)}, u32[]{:S(2)}) copy-start(f32[64,6,1,256]{3,0,1,2:T(8,128)} %copy-done.3) | copy-start | bytes 1179652
  90.1 119.1 %collective-permute-start.6 = (f32[2,32,512]{2,1,0:T(8,128)}, f32[2,32,512]{2,1,0:T(8,128)}, u32[]{:S(2)}, u32[]{:S(2)}) collective-permute-start(f32[2,32,512]{2,1,0:T(8,128)} %get-tuple-element.66), channel_id=1, source_target_pairs={{0,32},{32,64},{64,96},{96,128},{128,160},{160,192},{192,224},{224... | collective-permute-start | bytes 393224 | tf_op jit(solution)/shard_map/ppermute | solution.py:17
  93.8 118.8 %collective-permute-start.7 = (f32[2,32,512]{2,1,0:T(8,128)}, f32[2,32,512]{2,1,0:T(8,128)}, u32[]{:S(2)}, u32[]{:S(2)}) collective-permute-start(f32[2,32,512]{2,1,0:T(8,128)} %get-tuple-element.65), channel_id=1, source_target_pairs={{32,0},{64,32},{96,64},{128,96},{160,128},{192,160},{224,192},{256... | collective-permute-start | bytes 393224 | tf_op jit(solution)/shard_map/ppermute | solution.py:19
  212.5 7.3 %copy-start.16 = (f32[3,2,32,1536]{3,2,0,1:T(8,128)S(1)}, f32[3,2,32,1536]{3,2,0,1:T(8,128)}, u32[]{:S(2)}) copy-start(f32[3,2,32,1536]{3,2,0,1:T(8,128)} %copy-done.15) | copy-start | bytes 3538948
where the time goes:
time: 223 us; the launch traced here: 222 us
  blocking collectives  107 us (48%)
  local copies, waits for them, and re-layouts  43.2 us (19%)
  starting transfers between devices  38.4 us (17%)
  other arithmetic  17 us (8%)
  matrix products  15.1 us (7%)
    psum x1, blocking collectives, per_device(): filter_grad = lax.psum(local_grad, ('patch', 'map')) * scale  107 us
    ppermute x4, starting transfers between devices, extended_2(): lax.ppermute(head, axis, [((i + 1) % count, i) for i in range(count)])  26.1 us
    ppermute x4, starting transfers between devices, extended_2(): lax.ppermute(tail, axis, [(i, (i + 1) % count) for i in range(count)])  12.2 us
    another operation x4, local copies, waits for them, and re-layouts  6 us
    dot_general x2, matrix products, offset_sums(): jnp.einsum('uje,nujq->nueq', offset_mask.astype(jnp.float32), contrib, pr...  4.57 us
    convert_element_type x3, local copies, waits for them, and re-layouts, per_device(): x_one = forward_apply(maps).astype(jnp.bfloat16)  4.53 us
  transfers between devices with their start and end apart: 8, of which 0 were waited for; matrix products, arithmetic and copies ran while one was open for 17% of the time, Pallas kernels for 0%

commit v1 on v0

--- a/solution.py
+++ b/solution.py
@@ -1,3 +1,4 @@
+import functools
 import math
 import jax
 import jax.numpy as jnp
@@ -5,6 +6,15 @@
 from jax.sharding import PartitionSpec as P
 
 REACH = 2
+
+
+def stages_all_reach(x_in, along_axis, axis_tag):
+    for no in (along_axis, axis_tag):
+        x_in = lax.psum(x_in, no)
+    return x_in
+
+
+meet_inputs_up = functools.partial(stages_all_reach, along_axis="patch", axis_tag="map")
 
 
 def extended_2(cells, sides, width):
@@ -100,7 +110,7 @@
     )
     scale = 1.0 / math.sqrt(map_count * lax.axis_size("map") * pix_count * patch_count)
     local_grad = jnp.einsum("kmcp,mop->kco", terms, cotangent, preferred_element_type=jnp.float32)
-    filter_grad = lax.psum(local_grad, ("patch", "map")) * scale
+    filter_grad = meet_inputs_up(local_grad) * scale
     return (output, input_grad, filter_grad)
 
 

time: 223 us -> 310 us (1.39)
  the two profiles are of different devices: /device:TPU:1 before, /device:TPU:2 now
where the time goes in v1:
time: 310 us; the launch traced here: 309 us
  blocking collectives  195 us (63%)
  local copies, waits for them, and re-layouts  43.3 us (14%)
  starting transfers between devices  36.8 us (12%)
  other arithmetic  17 us (5%)
  matrix products  15.1 us (5%)
    psum x2, blocking collectives, stages_all_reach(): x_in = lax.psum(x_in, no)  195 us
    ppermute x4, starting transfers between devices, extended_2(): lax.ppermute(head, axis, [((i + 1) % count, i) for i in range(count)])  29.2 us
    ppermute x4, starting transfers between devices, extended_2(): lax.ppermute(tail, axis, [(i, (i + 1) % count) for i in range(count)])  7.64 us
  transfers between devices with their start and end apart: 8, of which 0 were waited for; matrix products, arithmetic and copies ran while one was open for 12% of the time, Pallas kernels for 0%

profile of v1, /device:TPU:2, one launch (start us, length us, event | category | flops | bytes accessed | tf_op | source)
XLA Modules:
  0.0 308.6 jit_solution(4678187027366399584)
XLA Ops:
  4.6 2.3 convolution_bitcast_fusion.3
  6.9 1.8 fusion.56
  10.8 1.8 reshape.181
  12.6 1.8 fusion.58
  14.4 1.9 collective-permute-start.4
  16.3 7.3 %collective-permute-start.5 = (f32[2,32,512]{2,1,0:T(8,128)}, f32[2,32,512]{2,1,0:T(8,128)}, u32[]{:S(2)}, u32[]{:S(2)}) collective-permute-start(f32[2,32,512]{2,1,0:T(8,128)} %get-tuple-element.67), channel_id=1, source_target_pairs={{32,0},{64,32},{96,64},{128,96},{160,128},{192,160},{224,192},{256... | collective-permute-start | bytes 393224 | tf_op jit(solution)/shard_map/ppermute | solution.py:29
  25.1 1.9 collective-permute-start
  27.0 7.3 %collective-permute-start.1 = (bf16[2,32,512]{2,1,0:T(8,128)(2,1)}, bf16[2,32,512]{2,1,0:T(8,128)(2,1)}, u32[]{:S(2)}, u32[]{:S(2)}) collective-permute-start(bf16[2,32,512]{2,1,0:T(8,128)(2,1)} %get-tuple-element.72), channel_id=1, source_target_pairs={{32,0},{64,32},{96,64},{128,96},{160,128},{192,160},{224,192},{256... | collective-permute-start | bytes 196616 | tf_op jit(solution)/shard_map/ppermute | solution.py:29
  34.3 1.8 slice.264
  37.0 1.9 squeeze.35
  45.0 1.9 convert_element_type.73
  46.9 1.9 convert_element_type.72
  50.3 1.9 collective-permute-start.2
  52.2 7.4 %collective-permute-start.3 = (bf16[2,32,512]{2,1,0:T(8,128)(2,1)}, bf16[2,32,512]{2,1,0:T(8,128)(2,1)}, u32[]{:S(2)}, u32[]{:S(2)}) collective-permute-start(bf16[2,32,512]{2,1,0:T(8,128)(2,1)} %get-tuple-element.70), channel_id=1, source_target_pairs={{32,0},{64,32},{96,64},{128,96},{160,128},{192,160},{224,192},{256... | collective-permute-start | bytes 196616 | tf_op jit(solution)/shard_map/ppermute | solution.py:29
  59.7 1.7 reshape.182
  61.3 1.7 fusion.44
  67.2 2.3 convolution_bitcast_fusion.2
  69.5 1.8 fusion.55
  81.3 2.0 convolution_bitcast_fusion.6
  85.1 1.9 reshape.184
  87.0 1.7 fusion.57
  88.7 1.9 collective-permute-start.6
  90.6 1.8 slice.279
  92.4 7.2 %collective-permute-start.7 = (f32[2,32,512]{2,1,0:T(8,128)}, f32[2,32,512]{2,1,0:T(8,128)}, u32[]{:S(2)}, u32[]{:S(2)}) collective-permute-start(f32[2,32,512]{2,1,0:T(8,128)} %get-tuple-element.65), channel_id=1, source_target_pairs={{32,0},{64,32},{96,64},{128,96},{160,128},{192,160},{224,192},{256... | collective-permute-start | bytes 393224 | tf_op jit(solution)/shard_map/ppermute | solution.py:29
  99.6 66.2 %psum.14 = f32[3,32,32]{2,1,0:T(8,128)} all-reduce(f32[3,32,32]{2,1,0:T(8,128)} %convolution_bitcast_fusion.6), channel_id=1, replica_groups=mesh['patch'=16,'map'=32] {'patch'}, use_global_device_ids=true, to_apply=%region_0.1 | all-reduce | flops 3072 | bytes 24576 | tf_op jit(solution)/shard_map/psum | solution.py:13
  165.8 128.9 %psum.15 = f32[3,32,32]{2,1,0:T(8,128)} all-reduce(f32[3,32,32]{2,1,0:T(8,128)} %psum.14), channel_id=1, replica_groups=mesh['patch'=16,'map'=32] {'map'}, use_global_device_ids=true, to_apply=%region_1.2 | all-reduce | flops 3072 | bytes 24576 | tf_op jit(solution)/shard_map/psum | solution.py:13
  296.2 1.7 reshape.185
  297.8 1.7 fusion.42
  299.5 1.7 reshape.186
  302.9 2.0 copy.42
  304.9 1.9 reshape.187
  306.8 1.7 fusion.20
  (110 shorter events, 34.9 us)
Async XLA Ops:
  0.6 3.5 %copy-start = (bf16[6,3,256,256]{3,2,1,0:T(8,128)(2,1)S(1)}, bf16[6,3,256,256]{3,2,1,0:T(8,128)(2,1)}, u32[]{:S(2)}) copy-start(bf16[6,3,256,256]{3,2,1,0:T(8,128)(2,1)} %param.15) | copy-start | bytes 7077892
  2.8 1.0 copy-start.15
  8.8 27.2 %copy-start.7 = (f32[64,6,256]{2,0,1:T(8,128)}, f32[64,6,256]{2,0,1:T(8,128)S(1)}, u32[]{:S(2)}) copy-start(f32[64,6,256]{2,0,1:T(8,128)S(1)} %get-tuple-element.73) | copy-start | bytes 1179652
  8.9 27.2 %copy-start.9 = (f32[64,6,256]{2,0,1:T(8,128)}, f32[64,6,256]{2,0,1:T(8,128)S(1)}, u32[]{:S(2)}) copy-start(f32[64,6,256]{2,0,1:T(8,128)S(1)} %get-tuple-element.74) | copy-start | bytes 1179652
  8.9 0.9 copy-start.11
  8.9 0.9 copy-start.13
  12.6 23.5 %copy-start.12 = (f32[64,6,256]{2,0,1:T(8,128)S(1)}, f32[64,6,256]{2,0,1:T(8,128)}, u32[]{:S(2)}) copy-start(f32[64,6,256]{2,0,1:T(8,128)} %copy-done.11) | copy-start | bytes 1179652
  12.6 23.5 %copy-start.14 = (f32[64,6,256]{2,0,1:T(8,128)S(1)}, f32[64,6,256]{2,0,1:T(8,128)}, u32[]{:S(2)}) copy-start(f32[64,6,256]{2,0,1:T(8,128)} %copy-done.13) | copy-start | bytes 1179652
  14.4 45.3 %collective-permute-start.4 = (f32[2,32,512]{2,1,0:T(8,128)}, f32[2,32,512]{2,1,0:T(8,128)}, u32[]{:S(2)}, u32[]{:S(2)}) collective-permute-start(f32[2,32,512]{2,1,0:T(8,128)} %get-tuple-element.68), channel_id=1, source_target_pairs={{0,32},{32,64},{64,96},{96,128},{128,160},{160,192},{192,224},{224... | collective-permute-start | bytes 393224 | tf_op jit(solution)/shard_map/ppermute | solution.py:27
  16.3 46.7 %collective-permute-start.5 = (f32[2,32,512]{2,1,0:T(8,128)}, f32[2,32,512]{2,1,0:T(8,128)}, u32[]{:S(2)}, u32[]{:S(2)}) collective-permute-start(f32[2,32,512]{2,1,0:T(8,128)} %get-tuple-element.67), channel_id=1, source_target_pairs={{32,0},{64,32},{96,64},{128,96},{160,128},{192,160},{224,192},{256... | collective-permute-start | bytes 393224 | tf_op jit(solution)/shard_map/ppermute | solution.py:29
  25.1 13.8 %collective-permute-start = (bf16[2,32,512]{2,1,0:T(8,128)(2,1)}, bf16[2,32,512]{2,1,0:T(8,128)(2,1)}, u32[]{:S(2)}, u32[]{:S(2)}) collective-permute-start(bf16[2,32,512]{2,1,0:T(8,128)(2,1)} %get-tuple-element.71), channel_id=1, source_target_pairs={{0,32},{32,64},{64,96},{96,128},{128,160},{160,192},{192,224},{224... | collective-permute-start | bytes 196616 | tf_op jit(solution)/shard_map/ppermute | solution.py:27
  27.0 11.9 %collective-permute-start.1 = (bf16[2,32,512]{2,1,0:T(8,128)(2,1)}, bf16[2,32,512]{2,1,0:T(8,128)(2,1)}, u32[]{:S(2)}, u32[]{:S(2)}) collective-permute-start(bf16[2,32,512]{2,1,0:T(8,128)(2,1)} %get-tuple-element.72), channel_id=1, source_target_pairs={{32,0},{64,32},{96,64},{128,96},{160,128},{192,160},{224,192},{256... | collective-permute-start | bytes 196616 | tf_op jit(solution)/shard_map/ppermute | solution.py:29
  36.2 2.7 copy-start.18
  44.2 17.1 %copy-start.8 = (f32[64,6,256]{2,0,1:T(8,128)S(1)}, f32[64,6,256]{2,0,1:T(8,128)}, u32[]{:S(2)}) copy-start(f32[64,6,256]{2,0,1:T(8,128)} %copy-done.7) | copy-start | bytes 1179652
  44.2 17.1 %copy-start.10 = (f32[64,6,256]{2,0,1:T(8,128)S(1)}, f32[64,6,256]{2,0,1:T(8,128)}, u32[]{:S(2)}) copy-start(f32[64,6,256]{2,0,1:T(8,128)} %copy-done.9) | copy-start | bytes 1179652
  50.3 23.2 %collective-permute-start.2 = (bf16[2,32,512]{2,1,0:T(8,128)(2,1)}, bf16[2,32,512]{2,1,0:T(8,128)(2,1)}, u32[]{:S(2)}, u32[]{:S(2)}) collective-permute-start(bf16[2,32,512]{2,1,0:T(8,128)(2,1)} %get-tuple-element.69), channel_id=1, source_target_pairs={{0,32},{32,64},{64,96},{96,128},{128,160},{160,192},{192,224},{224... | collective-permute-start | bytes 196616 | tf_op jit(solution)/shard_map/ppermute | solution.py:27
  52.2 21.3 %collective-permute-start.3 = (bf16[2,32,512]{2,1,0:T(8,128)(2,1)}, bf16[2,32,512]{2,1,0:T(8,128)(2,1)}, u32[]{:S(2)}, u32[]{:S(2)}) collective-permute-start(bf16[2,32,512]{2,1,0:T(8,128)(2,1)} %get-tuple-element.70), channel_id=1, source_target_pairs={{32,0},{64,32},{96,64},{128,96},{160,128},{192,160},{224,192},{256... | collective-permute-start | bytes 196616 | tf_op jit(solution)/shard_map/ppermute | solution.py:29
  71.4 1.3 copy-start.1
  71.5 1.3 copy-start.3
  71.5 1.2 copy-start.5
  71.6 1.2 copy-start.6
  72.8 1.0 copy-start.17
  79.1 1.1 copy-start.19
  80.2 3.1 copy-start.22
  80.2 3.1 copy-start.23
  81.3 3.0 copy-start.20
  81.3 2.9 copy-start.21
  85.1 212.7 %copy-start.2 = (f32[64,6,1,256]{3,0,1,2:T(8,128)S(1)}, f32[64,6,1,256]{3,0,1,2:T(8,128)}, u32[]{:S(2)}) copy-start(f32[64,6,1,256]{3,0,1,2:T(8,128)} %copy-done.1) | copy-start | bytes 1179652
  85.1 212.7 %copy-start.4 = (f32[64,6,1,256]{3,0,1,2:T(8,128)S(1)}, f32[64,6,1,256]{3,0,1,2:T(8,128)}, u32[]{:S(2)}) copy-start(f32[64,6,1,256]{3,0,1,2:T(8,128)} %copy-done.3) | copy-start | bytes 1179652
  88.7 207.5 %collective-permute-start.6 = (f32[2,32,512]{2,1,0:T(8,128)}, f32[2,32,512]{2,1,0:T(8,128)}, u32[]{:S(2)}, u32[]{:S(2)}) collective-permute-start(f32[2,32,512]{2,1,0:T(8,128)} %get-tuple-element.66), channel_id=1, source_target_pairs={{0,32},{32,64},{64,96},{96,128},{128,160},{160,192},{192,224},{224... | collective-permute-start | bytes 393224 | tf_op jit(solution)/shard_map/ppermute | solution.py:27
  92.4 207.1 %collective-permute-start.7 = (f32[2,32,512]{2,1,0:T(8,128)}, f32[2,32,512]{2,1,0:T(8,128)}, u32[]{:S(2)}, u32[]{:S(2)}) collective-permute-start(f32[2,32,512]{2,1,0:T(8,128)} %get-tuple-element.65), channel_id=1, source_target_pairs={{32,0},{64,32},{96,64},{128,96},{160,128},{192,160},{224,192},{256... | collective-permute-start | bytes 393224 | tf_op jit(solution)/shard_map/ppermute | solution.py:29
  299.5 7.3 %copy-start.16 = (f32[3,2,32,1536]{3,2,0,1:T(8,128)S(1)}, f32[3,2,32,1536]{3,2,0,1:T(8,128)}, u32[]{:S(2)}) copy-start(f32[3,2,32,1536]{3,2,0,1:T(8,128)} %copy-done.15) | copy-start | bytes 3538948
